TPU v7x, 32 devices: a whole 2x2x4 slice. The times are simulated.
32 devices in a mesh: req: 8 (over z, y), ep: 4 (over x, core).
Axes of the slice: x: 2, y: 2, z: 4, core: 2. Of those that a mesh axis runs over, the one named last changes fastest.
Arguments:
- tokens: bfloat16 [4096, 1536], P(('req', 'ep')), may hold values from -6 to 6
- seg_ids: int32 [4096], P(('req', 'ep')), may hold values from 0 to 3, never falling along the last dimension, each value on 1 to 2048 neighbouring positions
- routes: int32 [4096, 8], P(('req', 'ep')), may hold values from 0 to 39, all different within a row; in each aligned block of 128 rows (0 to 127, 128 to 255, ...) at most 48 rows name the same one
- route_weights: float32 [4096, 8], P(('req', 'ep')), may hold values from 0.05 to 0.3
- norm1_gain: float32 [1536], replicated, may hold values from 0.5 to 1.5
- norm2_gain: float32 [1536], replicated, may hold values from 0.5 to 1.5
- w_query: bfloat16 [1536, 1536], P(None, 'ep')
- key_weight: bfloat16 [1536, 512], P(None, 'ep')
- value_weight: bfloat16 [1536, 512], P(None, 'ep'), may hold values from -0.15625 to 0.15625
- w_out_attn: bfloat16 [1536, 1536], P('ep'), may hold values from -0.15625 to 0.15625
- w_in: bfloat16 [40, 1536, 1024], P('ep'), may hold values from -0.15625 to 0.15625
- w_out: bfloat16 [40, 512, 1536], P('ep'), may hold values from -0.25 to 0.25
- paged_key_value_cache: bfloat16 [96, 8, 2, 64, 64], P('req', 'ep'), may hold values from -6 to 6
- page_table: int32 [64], replicated, may hold values from 0 to 95, as said below
Outputs:
- attn_out: bfloat16 [4096, 1536], P(('req', 'ep'))
- moe_out: bfloat16 [4096, 1536], P(('req', 'ep'))
- new_cache: bfloat16 [96, 8, 2, 64, 64], P('req', 'ep')
Inputs may be any that keep to these rules, and one draw needn't show every extreme that they name: `seg_ids`: segment ids never fall along the stream; the longest prompt holds exactly half of the 4096 tokens. `routes`: each token names 8 different experts; within the rows of one device no expert is named more than 48 times, a bound that some block reaches. `page_table`: entries are distinct.
All inputs are finite; a program needn't handle non-finite values.
Results may differ from a plain program's by a relative error of at most 0.017.
Values may be sent and summed in bfloat16 or wider, within the bound.
No kernel may reach another device: no remote copies, remote signals or barrier semaphores. Data moves between devices by JAX's collectives and lax.ppermute only.
A program may use at most 192 MiB of HBM per device.

v0:
```python
import jax
import jax.numpy as jnp
from jax import lax
from jax.sharding import PartitionSpec as P

HEAD_SIZE = 64
E = 40
PAGE_TOKENS = 64
CAP = 48
norm_eps = 1e-06
score_scale = 0.015625
residual_scale = 0.22
rope_base = 10000.0
neg_fill = -1e30


def rms_scale(rows, gain):
    mean_sq = jnp.mean(rows * rows, axis=-1, keepdims=True)
    return rows * lax.rsqrt(mean_sq + norm_eps) * gain


def positions_of(segments):
    tok_index = jnp.arange(segments.shape[0], dtype=jnp.int32)
    previous = jnp.concatenate([jnp.full((1,), -1, jnp.int32), segments[:-1]])
    starts = jnp.where(segments != previous, tok_index, 0)
    return tok_index - lax.cummax(starts, axis=0)


def rotary_apply(heads_in, token_positions):
    half_dim = heads_in.shape[-1] // 2
    inverse_freq = rope_base ** (
        -jnp.arange(half_dim, dtype=jnp.float32) * 2.0 / heads_in.shape[-1]
    )
    angles = token_positions.astype(jnp.float32)[:, None] * inverse_freq[None, :]
    cos_part = jnp.cos(angles)[:, None, :]
    sine_part = jnp.sin(angles)[:, None, :]
    first_half = heads_in[..., :half_dim]
    second_half = heads_in[..., half_dim:]
    return jnp.concatenate(
        [
            first_half * cos_part - second_half * sine_part,
            second_half * cos_part + first_half * sine_part,
        ],
        axis=-1,
    )


def body(
    tokens,
    seg_ids,
    routes,
    route_weights,
    norm1_gain,
    norm2_gain,
    w_query,
    key_weight,
    value_weight,
    w_out_attn,
    w_in,
    w_out,
    paged_key_value_cache,
    page_table,
):
    tok_dev = tokens.shape[0]
    ep_count = lax.axis_size("ep")
    group_len = tok_dev * ep_count
    req_pos = lax.axis_index("req")
    all_segs = lax.all_gather(seg_ids, ("req", "ep"), axis=0, tiled=True)
    all_pos = positions_of(all_segs)
    group_start = req_pos * group_len
    group_pos = lax.dynamic_slice_in_dim(all_pos, group_start, group_len)
    group_seg = lax.dynamic_slice_in_dim(all_segs, group_start, group_len)
    normed = rms_scale(tokens.astype(jnp.float32), norm1_gain).astype(jnp.bfloat16)
    joined = jnp.concatenate([w_query, key_weight, value_weight], axis=1)
    projected = jnp.dot(
        lax.all_gather(normed, "ep", axis=0, tiled=True), joined, preferred_element_type=jnp.float32
    )
    query_width = w_query.shape[1]
    kv_width = key_weight.shape[1]
    q_heads = query_width // HEAD_SIZE
    kv_heads = kv_width // HEAD_SIZE
    heads_ratio = q_heads // kv_heads
    query_rows = rotary_apply(
        projected[:, :query_width].reshape(group_len, q_heads, HEAD_SIZE), group_pos
    ).astype(jnp.bfloat16)
    key_matrix = (
        rotary_apply(
            projected[:, query_width : query_width + kv_width].reshape(
                group_len, kv_heads, HEAD_SIZE
            ),
            group_pos,
        )
        .astype(jnp.bfloat16)
        .reshape(group_len, kv_width)
    )
    value_rows = projected[:, query_width + kv_width :].astype(jnp.bfloat16)
    query_grouped = query_rows.reshape(group_len, kv_heads, heads_ratio, HEAD_SIZE).transpose(
        1, 2, 0, 3
    )
    pages_here = paged_key_value_cache.shape[0]
    page_first = req_pos * pages_here
    q_last = group_start + group_len - 1
    seg_low = group_seg[0]
    q_index = group_start + jnp.arange(group_len, dtype=jnp.int32)
    page_cells = kv_heads * 2 * PAGE_TOKENS * HEAD_SIZE
    cache_shape = paged_key_value_cache.shape
    local_pages = page_first + jnp.arange(pages_here, dtype=jnp.int32)
    begin_at = jnp.int32(0)
    run_max = jnp.full((kv_heads, heads_ratio, group_len), neg_fill, jnp.float32)
    run_sum = jnp.zeros((kv_heads, heads_ratio, group_len), jnp.float32)
    run_acc = jnp.zeros((kv_heads, heads_ratio, group_len, HEAD_SIZE), jnp.float32)
    cache_rows = paged_key_value_cache.reshape(pages_here, page_cells)
    key_piece = lax.all_gather(key_matrix, "req", axis=0, tiled=True)
    value_piece = lax.all_gather(value_rows, "req", axis=0, tiled=True)
    n_rows = key_piece.shape[0]
    piece_pages = n_rows // PAGE_TOKENS
    keys_paged = key_piece.reshape(piece_pages, PAGE_TOKENS, kv_heads, HEAD_SIZE).transpose(
        0, 2, 1, 3
    )
    values_paged = value_piece.reshape(piece_pages, PAGE_TOKENS, kv_heads, HEAD_SIZE).transpose(
        0, 2, 1, 3
    )
    fresh = jnp.stack([keys_paged, values_paged], axis=2).reshape(piece_pages, page_cells)
    match = local_pages[:, None] == page_table[None, :]
    placed = jnp.dot(match.astype(jnp.bfloat16), fresh, preferred_element_type=jnp.float32).astype(
        jnp.bfloat16
    )
    hit = jnp.any(match, axis=1)
    cache_rows = jnp.where(hit[:, None], placed, cache_rows)
    last_seg = lax.dynamic_index_in_dim(all_segs, begin_at + n_rows - 1, keepdims=False)
    needed = (begin_at <= q_last) & (last_seg >= seg_low)
    step_rows = min(n_rows, 1024)
    turns = n_rows // step_rows

    def attend(state_in):

        def one_block(turn_idx, state_now):
            block_max, block_sum, block_acc = state_now
            row_at = turn_idx * step_rows
            key_block = lax.dynamic_slice_in_dim(key_piece, row_at, step_rows).reshape(
                step_rows, kv_heads, HEAD_SIZE
            )
            value_block = lax.dynamic_slice_in_dim(value_piece, row_at, step_rows).reshape(
                step_rows, kv_heads, HEAD_SIZE
            )
            key_index = row_at + jnp.arange(step_rows, dtype=jnp.int32)
            key_segs = lax.dynamic_slice_in_dim(all_segs, row_at, step_rows)
            allowed = (group_seg[:, None] == key_segs[None, :]) & (
                key_index[None, :] <= q_index[:, None]
            )
            scores = (
                jnp.einsum(
                    "grqd,kgd->grqk", query_grouped, key_block, preferred_element_type=jnp.float32
                )
                * score_scale
            )
            masked = jnp.where(allowed, scores, neg_fill)
            new_max = jnp.maximum(block_max, jnp.max(masked, axis=-1))
            exponent = jnp.where(allowed, jnp.exp(masked - new_max[..., None]), 0.0)
            rescale = jnp.exp(block_max - new_max)
            new_sum = block_sum * rescale + jnp.sum(exponent, axis=-1)
            new_acc = block_acc * rescale[..., None] + jnp.einsum(
                "grqk,kgd->grqd",
                exponent.astype(jnp.bfloat16),
                value_block,
                preferred_element_type=jnp.float32,
            )
            return (new_max, new_sum, new_acc)

        return lax.fori_loop(0, turns, one_block, state_in)

    run_max, run_sum, run_acc = lax.cond(
        needed, attend, lambda state_in: state_in, (run_max, run_sum, run_acc)
    )
    run_max, run_sum, run_acc, cache_flat = (run_max, run_sum, run_acc, cache_rows)
    new_cache = cache_flat.reshape(cache_shape)
    head_out = (run_acc / run_sum[..., None]).astype(jnp.bfloat16)
    head_out = head_out.transpose(2, 0, 1, 3).reshape(group_len, query_width)
    attention = lax.psum_scatter(
        jnp.dot(head_out, w_out_attn, preferred_element_type=jnp.float32).astype(jnp.bfloat16),
        "ep",
        scatter_dimension=0,
        tiled=True,
    ).astype(jnp.float32)
    attn_out = attention.astype(jnp.bfloat16)
    moe_in = rms_scale(tokens.astype(jnp.float32) + residual_scale * attention, norm2_gain).astype(
        jnp.bfloat16
    )
    ffe_width = w_out.shape[1]
    exp_here = w_in.shape[0]
    expert_ids = jnp.arange(E, dtype=jnp.int32)
    shares = jnp.sum(
        jnp.where(routes[:, :, None] == expert_ids[None, None, :], route_weights[:, :, None], 0.0),
        axis=1,
    )
    rows_all = lax.all_gather(moe_in, "ep", axis=0, tiled=True)
    shares_all = lax.all_gather(shares, "ep", axis=0, tiled=True)
    first_expert = lax.axis_index("ep") * exp_here
    shares_here = lax.dynamic_slice_in_dim(shares_all, first_expert, exp_here, 1)
    total_rows = rows_all.shape[0]
    chosen = (shares_here > 0.0).astype(jnp.int32).reshape(ep_count, tok_dev, exp_here)
    slot_in = jnp.cumsum(chosen, axis=1) - 1
    source_ids = jnp.arange(ep_count, dtype=jnp.int32)[:, None, None]
    local_slot = (source_ids * CAP + slot_in).reshape(total_rows, exp_here)
    live = (chosen > 0).reshape(total_rows, exp_here)
    slot_ids = jnp.arange(ep_count * CAP, dtype=jnp.int32)
    dispatch = (local_slot.T[:, None, :] == slot_ids[None, :, None]) & live.T[:, None, :]
    arrived = jnp.einsum(
        "esr,rd->esd", dispatch.astype(jnp.bfloat16), rows_all, preferred_element_type=jnp.float32
    ).astype(jnp.bfloat16)
    gate_up = jnp.einsum("esd,edf->esf", arrived, w_in, preferred_element_type=jnp.float32)
    activated = (jax.nn.silu(gate_up[..., :ffe_width]) * gate_up[..., ffe_width:]).astype(
        jnp.bfloat16
    )
    result = jnp.einsum(
        "esf,efd->esd", activated, w_out, preferred_element_type=jnp.float32
    ).astype(jnp.bfloat16)
    slot_weight = jnp.sum(jnp.where(dispatch, shares_here.T[:, None, :], 0.0), axis=2)
    weighted = result.astype(jnp.float32) * slot_weight[..., None]
    partial_rows = jnp.einsum(
        "esr,esd->rd",
        dispatch.astype(jnp.float32),
        weighted,
        precision=lax.Precision.HIGHEST,
        preferred_element_type=jnp.float32,
    )
    moe_out = lax.psum_scatter(
        partial_rows.astype(jnp.bfloat16), "ep", scatter_dimension=0, tiled=True
    )
    return (attn_out, moe_out, new_cache)


def solution(mesh):
    in_specs = (
        P(("req", "ep"), None),
        P(("req", "ep")),
        P(("req", "ep"), None),
        P(("req", "ep"), None),
        P(),
        P(),
        P(None, "ep"),
        P(None, "ep"),
        P(None, "ep"),
        P("ep", None),
        P("ep", None, None),
        P("ep", None, None),
        P("req", "ep", None, None, None),
        P(),
    )
    out_specs = (P(("req", "ep"), None), P(("req", "ep"), None), P("req", "ep", None, None, None))
    return jax.shard_map(body, mesh=mesh, in_specs=in_specs, out_specs=out_specs, check_vma=False)
```

profile of v0, /device:TPU:0, one launch (start us, length us, event | category | flops | bytes accessed | tf_op | source)
XLA Modules:
  0.0 372.4 jit_solution(15703386580134532242)
XLA Ops:
  7.2 1.2 fusion.57
  8.5 1.9 fusion.59
  10.5 43.2 %all-gather = s32[32,1,128]{2,1,0:T(1,128)S(1)} all-gather(s32[1,1,128]{2,1,0:T(1,128)} %bitcast.115), channel_id=1, replica_groups=mesh['req'=8,'ep'=4] {'req','ep'}, dimensions={0}, use_global_device_ids=true | all-gather | bytes 16896 | tf_op jit(solution)/shard_map/all_gather | solution.py:68
  54.8 3.4 fusion.42
  62.6 1.2 slice.61
  64.3 30.8 %all-gather.8.cloned.1.call-done = bf16[4096,128]{0,1:T(8,128)(2,1)} async-done(((bf16[512,128]{0,1:T(8,128)(2,1)}), bf16[4096,128]{0,1:T(8,128)(2,1)}) %all-gather.8.cloned.1.call-update) | async-done | bytes 1048592 | tf_op jit(solution)/shard_map/all_gather | solution.py:113
  95.1 41.8 %all-gather.10.cloned.1.call-done = bf16[4096,128]{1,0:T(8,128)(2,1)} async-done(((bf16[512,128]{1,0:T(8,128)(2,1)}), bf16[4096,128]{1,0:T(8,128)(2,1)}) %all-gather.10.cloned.1.call-update) | async-done | bytes 1048592 | tf_op jit(solution)/shard_map/all_gather | solution.py:114
  136.9 99.9 %conditional.1 = (f32[2,3,512]{2,1,0:T(4,128)}, f32[2,3,512,64]{2,3,1,0:T(8,128)}) conditional(s32[]{:T(128)} %convert_element_type.66, () %tuple.30, (s32[]{:T(128)}, s32[512]{0:T(512)S(1)}, s32[512]{0:T(512)S(1)}, s32[4096]{0:T(1024)S(1)}, bf16[4096,128]{0,1:T(8,128)(2,1)}, /*index=5*/bf16[2,3,512,64]{2,3,1,0:T(8,128)(2,1)S(1)}, ...), branch_computations={%region_3.4_spmd, %region_4.9_spmd} | conditional | flops 848380416 | bytes 44134744 | solution.py:172
  136.9 99.9 %while.17 = (s32[]{:T(128)}, f32[2,3,512]{2,1,0:T(4,128)S(1)}, f32[2,3,512]{2,1,0:T(4,128)}, f32[2,3,512,64]{2,3,1,0:T(8,128)}, s32[512]{0:T(512)S(1)}, /*index=...) while((s32[]{:T(128)}, f32[2,3,512]{2,1,0:T(4,128)S(1)}, ...), condition=%wide.region_8.8_spmd.clone, body=%wide.region_5.7_spmd.clone.sunk | while | flops 848379904 | bytes 44130508 | solution.py:170
  137.8 1.0 constant_dynamic-slice_fusion.4
  138.7 6.7 %fusion.87 = (f32[2,3,512]{2,1,0:T(4,128)S(1)}, f32[2,1024,3,512]{3,1,2,0:T(8,128)}) fusion(pred[512,1024]{0,1:T(8,128)(4,1)S(1)} %compare_and_fusion.2, bf16[1024,2,64,1]{0,2,3,1:T(8,128)(2,1)S(1)} %bitcast.98, bf16[2,3,512,64]{2,3,1,0:T(8,128)(2,1)S(1)} %get-tuple-element.398), kind=kOutput, calls=%fused_computation.2.clone.1 | convolution fusion | flops 412087296 | bytes 13774848 | tf_op jit(solution)/shard_map/cond/branch_1_fun/while/body/eval_jaxpr/grqd,kgd->grqk/dot_general | solution.py:152
  145.4 6.5 %fusion.88 = f32[2,3,512]{2,1,0:T(4,128)S(1)} fusion(f32[2,1024,3,512]{3,1,2,0:T(8,128)} %get-tuple-element.359, f32[2,3,512]{2,1,0:T(4,128)S(1)} %select_maximum_fusion.2, pred[512,1024]{0,1:T(8,128)(4,1)S(1)} %compare_and_fusion.2), kind=kLoop, calls=%fused_computation.4.clone.1 | loop fusion | flops 15725568 | bytes 13131776 | tf_op jit(solution)/shard_map/cond/branch_1_fun/while/body/eval_jaxpr/reduce_sum | solution.py:161
  153.7 7.4 %fusion.90 = f32[2,3,512,64]{2,3,1,0:T(8,128)} fusion(bf16[1024,2,64,1]{0,2,3,1:T(8,128)(2,1)S(1)} %bitcast.101, f32[2,1024,3,512]{3,1,2,0:T(8,128)} %get-tuple-element.359, f32[2,3,512]{2,1,0:T(4,128)S(1)} %select_maximum_fusion.2, pred[512,1024]{0,1:T(8,128)(4,1)S(1)} %compare_and_fusion.2, f32[2,3,512,64]{2,3,1,0:T(8,128)} %get-tuple-element.379, ...), kind=kOutput, calls=%fused_computation.8.clone.1 | convolution fusion | flops 418971648 | bytes 14966785 | tf_op jit(solution)/shard_map/cond/branch_1_fun/while/body/eval_jaxpr/grqk,kgd->grqd/dot_general | solution.py:162
  162.0 1.0 constant_dynamic-slice_fusion.4
  163.0 6.7 %fusion.87 = (f32[2,3,512]{2,1,0:T(4,128)S(1)}, f32[2,1024,3,512]{3,1,2,0:T(8,128)}) fusion(pred[512,1024]{0,1:T(8,128)(4,1)S(1)} %compare_and_fusion.2, bf16[1024,2,64,1]{0,2,3,1:T(8,128)(2,1)S(1)} %bitcast.98, bf16[2,3,512,64]{2,3,1,0:T(8,128)(2,1)S(1)} %get-tuple-element.398), kind=kOutput, calls=%fused_computation.2.clone.1 | convolution fusion | flops 412087296 | bytes 13774848 | tf_op jit(solution)/shard_map/cond/branch_1_fun/while/body/eval_jaxpr/grqd,kgd->grqk/dot_general | solution.py:152
  169.7 6.5 %fusion.88 = f32[2,3,512]{2,1,0:T(4,128)S(1)} fusion(f32[2,1024,3,512]{3,1,2,0:T(8,128)} %get-tuple-element.359, f32[2,3,512]{2,1,0:T(4,128)S(1)} %select_maximum_fusion.2, pred[512,1024]{0,1:T(8,128)(4,1)S(1)} %compare_and_fusion.2), kind=kLoop, calls=%fused_computation.4.clone.1 | loop fusion | flops 15725568 | bytes 13131776 | tf_op jit(solution)/shard_map/cond/branch_1_fun/while/body/eval_jaxpr/reduce_sum | solution.py:161
  176.2 1.4 fusion.89
  178.7 7.6 %fusion.90 = f32[2,3,512,64]{2,3,1,0:T(8,128)} fusion(bf16[1024,2,64,1]{0,2,3,1:T(8,128)(2,1)S(1)} %bitcast.101, f32[2,1024,3,512]{3,1,2,0:T(8,128)} %get-tuple-element.359, f32[2,3,512]{2,1,0:T(4,128)S(1)} %select_maximum_fusion.2, pred[512,1024]{0,1:T(8,128)(4,1)S(1)} %compare_and_fusion.2, f32[2,3,512,64]{2,3,1,0:T(8,128)} %get-tuple-element.379, ...), kind=kOutput, calls=%fused_computation.8.clone.1 | convolution fusion | flops 418971648 | bytes 14966785 | tf_op jit(solution)/shard_map/cond/branch_1_fun/while/body/eval_jaxpr/grqk,kgd->grqd/dot_general | solution.py:162
  187.2 1.0 constant_dynamic-slice_fusion.4
  188.2 6.7 %fusion.87 = (f32[2,3,512]{2,1,0:T(4,128)S(1)}, f32[2,1024,3,512]{3,1,2,0:T(8,128)}) fusion(pred[512,1024]{0,1:T(8,128)(4,1)S(1)} %compare_and_fusion.2, bf16[1024,2,64,1]{0,2,3,1:T(8,128)(2,1)S(1)} %bitcast.98, bf16[2,3,512,64]{2,3,1,0:T(8,128)(2,1)S(1)} %get-tuple-element.398), kind=kOutput, calls=%fused_computation.2.clone.1 | convolution fusion | flops 412087296 | bytes 13774848 | tf_op jit(solution)/shard_map/cond/branch_1_fun/while/body/eval_jaxpr/grqd,kgd->grqk/dot_general | solution.py:152
  194.9 6.5 %fusion.88 = f32[2,3,512]{2,1,0:T(4,128)S(1)} fusion(f32[2,1024,3,512]{3,1,2,0:T(8,128)} %get-tuple-element.359, f32[2,3,512]{2,1,0:T(4,128)S(1)} %select_maximum_fusion.2, pred[512,1024]{0,1:T(8,128)(4,1)S(1)} %compare_and_fusion.2), kind=kLoop, calls=%fused_computation.4.clone.1 | loop fusion | flops 15725568 | bytes 13131776 | tf_op jit(solution)/shard_map/cond/branch_1_fun/while/body/eval_jaxpr/reduce_sum | solution.py:161
  201.4 1.4 fusion.89
  203.9 7.6 %fusion.90 = f32[2,3,512,64]{2,3,1,0:T(8,128)} fusion(bf16[1024,2,64,1]{0,2,3,1:T(8,128)(2,1)S(1)} %bitcast.101, f32[2,1024,3,512]{3,1,2,0:T(8,128)} %get-tuple-element.359, f32[2,3,512]{2,1,0:T(4,128)S(1)} %select_maximum_fusion.2, pred[512,1024]{0,1:T(8,128)(4,1)S(1)} %compare_and_fusion.2, f32[2,3,512,64]{2,3,1,0:T(8,128)} %get-tuple-element.379, ...), kind=kOutput, calls=%fused_computation.8.clone.1 | convolution fusion | flops 418971648 | bytes 14966785 | tf_op jit(solution)/shard_map/cond/branch_1_fun/while/body/eval_jaxpr/grqk,kgd->grqd/dot_general | solution.py:162
  212.4 1.0 constant_dynamic-slice_fusion.4
  213.4 6.7 %fusion.87 = (f32[2,3,512]{2,1,0:T(4,128)S(1)}, f32[2,1024,3,512]{3,1,2,0:T(8,128)}) fusion(pred[512,1024]{0,1:T(8,128)(4,1)S(1)} %compare_and_fusion.2, bf16[1024,2,64,1]{0,2,3,1:T(8,128)(2,1)S(1)} %bitcast.98, bf16[2,3,512,64]{2,3,1,0:T(8,128)(2,1)S(1)} %get-tuple-element.398), kind=kOutput, calls=%fused_computation.2.clone.1 | convolution fusion | flops 412087296 | bytes 13774848 | tf_op jit(solution)/shard_map/cond/branch_1_fun/while/body/eval_jaxpr/grqd,kgd->grqk/dot_general | solution.py:152
  220.1 6.5 %fusion.88 = f32[2,3,512]{2,1,0:T(4,128)S(1)} fusion(f32[2,1024,3,512]{3,1,2,0:T(8,128)} %get-tuple-element.359, f32[2,3,512]{2,1,0:T(4,128)S(1)} %select_maximum_fusion.2, pred[512,1024]{0,1:T(8,128)(4,1)S(1)} %compare_and_fusion.2), kind=kLoop, calls=%fused_computation.4.clone.1 | loop fusion | flops 15725568 | bytes 13131776 | tf_op jit(solution)/shard_map/cond/branch_1_fun/while/body/eval_jaxpr/reduce_sum | solution.py:161
  226.6 1.4 fusion.89
  228.0 1.0 constant_dynamic-slice_fusion.5
  229.1 7.6 %fusion.90 = f32[2,3,512,64]{2,3,1,0:T(8,128)} fusion(bf16[1024,2,64,1]{0,2,3,1:T(8,128)(2,1)S(1)} %bitcast.101, f32[2,1024,3,512]{3,1,2,0:T(8,128)} %get-tuple-element.359, f32[2,3,512]{2,1,0:T(4,128)S(1)} %select_maximum_fusion.2, pred[512,1024]{0,1:T(8,128)(4,1)S(1)} %compare_and_fusion.2, f32[2,3,512,64]{2,3,1,0:T(8,128)} %get-tuple-element.379, ...), kind=kOutput, calls=%fused_computation.8.clone.1 | convolution fusion | flops 418971648 | bytes 14966785 | tf_op jit(solution)/shard_map/cond/branch_1_fun/while/body/eval_jaxpr/grqk,kgd->grqd/dot_general | solution.py:162
  236.8 1.3 divide_convert_fusion
  238.1 2.2 convolution_convert_fusion.1
  240.3 27.0 %reduce-scatter.3.cloned.1.call-done = bf16[128,1536]{1,0:T(8,128)(2,1)} async-done(((bf16[512,1536]{1,0:T(8,128)(2,1)}), bf16[128,1536]{1,0:T(8,128)(2,1)}) %reduce-scatter.3.cloned.1.call-update) | async-done | bytes 393232 | tf_op jit(solution)/shard_map/reduce_scatter | solution.py:179
  267.3 1.2 multiply_reduce_fusion
  268.6 1.9 multiply_convert_fusion
  270.6 5.5 %all_gather.22 = f32[512,40]{0,1:T(8,128)S(1)} all-gather(f32[128,40]{0,1:T(8,128)S(1)} %select_reduce_fusion.1), channel_id=1, replica_groups=mesh['req'=8,'ep'=4] {'ep'}, dimensions={0}, use_global_device_ids=true | all-gather | bytes 102400 | tf_op jit(solution)/shard_map/all_gather | solution.py:197
  277.8 12.5 %all-gather.12.cloned.1.call-done = bf16[512,1536]{1,0:T(8,128)(2,1)} async-done(((bf16[128,1536]{1,0:T(8,128)(2,1)}), bf16[512,1536]{1,0:T(8,128)(2,1)}) %all-gather.12.cloned.1.call-update) | async-done | bytes 1572880 | tf_op jit(solution)/shard_map/all_gather | solution.py:196
  290.4 17.3 %fusion.19 = f32[10,192,1024]{2,1,0:T(8,128)} fusion(bf16[10,1536,1024]{2,1,0:T(8,128)(2,1)} %param.28, s32[10,512]{1,0:T(8,128)S(1)} %copy.55, pred[10,512]{1,0:T(8,128)(4,1)S(1)} %get-tuple-element.283, bf16[512,1536]{1,0:T(8,128)(2,1)} %all-gather.12.cloned.1.call-done), kind=kOutput, calls=%fused_computation.28 | convolution fusion | flops 9064611840 | bytes 40920064 | tf_op jit(solution)/shard_map/esd,edf->esf/dot_general | solution.py:211
  307.6 13.6 %fusion.40 = bf16[10,192,1536]{2,1,0:T(8,128)(2,1)} fusion(bf16[10,512,1536]{2,1,0:T(8,128)(2,1)} %param.29, f32[10,192,1024]{2,1,0:T(8,128)} %fusion.19), kind=kOutput, calls=%fused_computation.41 | convolution fusion | flops 3025797120 | bytes 29491200 | tf_op jit(solution)/shard_map/esf,efd->esd/dot_general | solution.py:215
  321.2 15.9 %fusion.35 = bf16[512,1536]{1,0:T(8,128)(2,1)} fusion(f32[10,192]{1,0:T(8,128)S(1)} %select_reduce_fusion, bf16[10,192,1536]{2,1,0:T(8,128)(2,1)} %fusion.40, s32[10,512]{1,0:T(8,128)S(1)} %copy.55, pred[10,512]{1,0:T(8,128)(4,1)S(1)} %get-tuple-element.283), kind=kOutput, calls=%fused_computation.38 | convolution fusion | flops 18128044032 | bytes 7504384 | tf_op jit(solution)/shard_map/esr,esd->rd/dot_general | solution.py:220
  337.2 1.5 reshape.181
  338.9 2.3 reshape.178
  341.2 3.0 copy.56
  345.6 1.1 copy-done.2
  346.7 2.7 pad_maximum_fusion
  349.4 5.0 %reshape.180 = bf16[64,16384]{1,0:T(8,128)(2,1)S(1)} reshape(bf16[64,2,2,64,64]{4,3,2,1,0:T(8,128)(2,1)} %pad_maximum_fusion) | data formatting | bytes 4194304 | tf_op jit(solution)/shard_map/reshape | solution.py:123
  354.4 2.3 fusion.13
  356.7 2.7 reshape.182
  359.4 6.1 %reduce-scatter.5.cloned.1.call-done = bf16[128,1536]{1,0:T(8,128)(2,1)} async-done(((bf16[512,1536]{1,0:T(8,128)(2,1)}), bf16[128,1536]{1,0:T(8,128)(2,1)}) %reduce-scatter.5.cloned.1.call-update) | async-done | bytes 393232 | tf_op jit(solution)/shard_map/reduce_scatter | solution.py:227
  (106 shorter events, 15.8 us)
Async XLA Ops:
  7.2 230.9 %copy-start = (bf16[384,1536]{1,0:T(8,128)(2,1)S(1)}, bf16[384,1536]{1,0:T(8,128)(2,1)}, u32[]{:S(2)}) copy-start(bf16[384,1536]{1,0:T(8,128)(2,1)} %param.27) | copy-start | bytes 3538948
  7.2 47.6 %all-gather.6.cloned.1.call-start = ((), (), s32[]{:S(2)}) async-start(), calls=%async_computation.2 | async-start | bytes 1966080 | tf_op jit(solution)/shard_map/all_gather | solution.py:76
  10.4 84.7 %all-gather.8.cloned.1.call-start = ((), (), s32[]{:S(2)}) async-start(), calls=%async_computation.3 | async-start | bytes 1179648 | tf_op jit(solution)/shard_map/all_gather | solution.py:113
  58.2 4.4 %copy-start.6 = (f32[512,640]{1,0:T(8,128)}, f32[512,640]{1,0:T(8,128)S(1)}, u32[]{:S(2)}) copy-start(f32[512,640]{1,0:T(8,128)S(1)} %fusion.42) | copy-start | bytes 3932164
  59.3 77.5 %all-gather.10.cloned.1.call-start = ((), (), s32[]{:S(2)}) async-start(), calls=%async_computation.4 | async-start | bytes 1179648 | tf_op jit(solution)/shard_map/all_gather | solution.py:114
  60.1 207.3 %reduce-scatter.3.cloned.1.call-start = ((), (), s32[]{:S(2)}) async-start(), calls=%async_computation.5 | async-start | bytes 1966080 | tf_op jit(solution)/shard_map/reduce_scatter | solution.py:179
  236.7 30.6 %copy-start.3 = (bf16[128,1536]{1,0:T(8,128)(2,1)S(1)}, bf16[128,1536]{1,0:T(8,128)(2,1)}, u32[]{:S(2)}) copy-start(bf16[128,1536]{1,0:T(8,128)(2,1)} %param.18) | copy-start | bytes 1179652
  236.7 31.8 %copy-start.8 = (f32[1536]{0:T(1024)S(1)}, f32[1536]{0:T(1024)}, u32[]{:S(2)}) copy-start(f32[1536]{0:T(1024)} %param.23) | copy-start | bytes 18436
  236.7 33.8 %copy-start.9 = (f32[128,8]{0,1:T(8,128)S(1)}, f32[128,8]{0,1:T(8,128)}, u32[]{:S(2)}) copy-start(f32[128,8]{0,1:T(8,128)} %param.21) | copy-start | bytes 12292
  236.8 33.8 %copy-start.10 = (s32[128,8]{0,1:T(8,128)S(1)}, s32[128,8]{0,1:T(8,128)}, u32[]{:S(2)}) copy-start(s32[128,8]{0,1:T(8,128)} %param.20) | copy-start | bytes 12292
  240.3 50.1 %all-gather.12.cloned.1.call-start = ((), (), s32[]{:S(2)}) async-start(), calls=%async_computation.6 | async-start | bytes 1966080 | tf_op jit(solution)/shard_map/all_gather | solution.py:196
  270.5 95.0 %reduce-scatter.5.cloned.1.call-start = ((), (), s32[]{:S(2)}) async-start(), calls=%async_computation.7 | async-start | bytes 1966080 | tf_op jit(solution)/shard_map/reduce_scatter | solution.py:227
  321.2 16.0 %copy-start.7 = (bf16[12,2,2,64,64]{4,3,2,1,0:T(8,128)(2,1)S(1)}, bf16[12,2,2,64,64]{4,3,2,1,0:T(8,128)(2,1)}, u32[]{:S(2)}) copy-start(bf16[12,2,2,64,64]{4,3,2,1,0:T(8,128)(2,1)} %param.30) | copy-start | bytes 1179652
  321.2 17.5 %copy-start.11 = (s32[64]{0:T(128)S(1)}, s32[64]{0:T(128)}, u32[]{:S(2)}) copy-start(s32[64]{0:T(128)} %param.31) | copy-start | bytes 772
  321.2 17.7 %copy-start.4 = (bf16[4096,128]{0,1:T(8,128)(2,1)S(1)}, bf16[4096,128]{0,1:T(8,128)(2,1)}, u32[]{:S(2)}) copy-start(bf16[4096,128]{0,1:T(8,128)(2,1)} %all-gather.8.cloned.1.call-done) | copy-start | bytes 3145732
  341.2 3.0 copy-start.5
  345.0 1.7 copy-start.2
  346.7 18.9 %copy-start.1 = (bf16[384,1536]{1,0:T(8,128)(2,1)S(1)}, bf16[384,1536]{1,0:T(8,128)(2,1)}, u32[]{:S(2)}) copy-start(bf16[384,1536]{1,0:T(8,128)(2,1)} %param.27) | copy-start | bytes 3538948
Sparse Core Ops, SparseCore 0:
  10.5 22.3 all-gather.5
  59.4 35.5 all-gather.7
  97.8 39.0 all-gather.9
  240.4 26.9 reduce-scatter.2
  270.7 19.6 all-gather.11
  337.3 28.1 reduce-scatter.4
where the time goes:
time: 373 us; the launch traced here: 372 us
  waiting for transfers between devices  118 us (32%)
  matrix products  112 us (30%)
  blocking collectives  48.7 us (13%)
  other arithmetic  48.2 us (13%)
  local copies, waits for them, and re-layouts  29.4 us (8%)
  between operations  15.7 us (4%)
    all_gather x1, blocking collectives, body(): all_segs = lax.all_gather(seg_ids, ('req', 'ep'), axis=0, tiled=True)  43.2 us
    all_gather x1, waiting for transfers between devices, body(): value_piece = lax.all_gather(value_rows, 'req', axis=0, tiled=True)  41.8 us
    all_gather x1, waiting for transfers between devices, body(): key_piece = lax.all_gather(key_matrix, 'req', axis=0, tiled=True)  30.8 us
    dot_general x4, matrix products, one_block(): jnp.einsum('grqk,kgd->grqd', exponent.astype(jnp.bfloat16), value_block,...  30.3 us
    reduce_scatter x1, waiting for transfers between devices, body(): lax.psum_scatter(jnp.dot(head_out, w_out_attn, preferred_element_type=jnp...  27 us
    dot_general x4, matrix products, one_block(): jnp.einsum('grqd,kgd->grqk', query_grouped, key_block, preferred_element_...  26.7 us
    reduce_sum x4, other arithmetic, one_block(): new_sum = block_sum * rescale + jnp.sum(exponent, axis=-1)  26.2 us
    dot_general x1, matrix products, body(): jnp.einsum('esd,edf->esf', arrived, w_in, preferred_element_type=jnp.floa...  17.3 us
  transfers between devices with their start and end apart: 6, of which 5 were waited for; matrix products, arithmetic and copies ran while one was open for 7% of the time, Pallas kernels for 0%

commit v1 on v0

--- a/solution.py
+++ b/solution.py
@@ -110,8 +110,14 @@
     run_sum = jnp.zeros((kv_heads, heads_ratio, group_len), jnp.float32)
     run_acc = jnp.zeros((kv_heads, heads_ratio, group_len, HEAD_SIZE), jnp.float32)
     cache_rows = paged_key_value_cache.reshape(pages_here, page_cells)
-    key_piece = lax.all_gather(key_matrix, "req", axis=0, tiled=True)
-    value_piece = lax.all_gather(value_rows, "req", axis=0, tiled=True)
+    sizes_choose = lambda x_local, device_axis, block_in: jnp.split(
+        lax.all_gather(
+            jnp.concatenate([x_local, block_in], 1), axis_name=device_axis, axis=0, tiled=True
+        ),
+        [x_local.shape[1]],
+        1,
+    )
+    key_piece, value_piece = sizes_choose(key_matrix, "req", block_in=value_rows)
     n_rows = key_piece.shape[0]
     piece_pages = n_rows // PAGE_TOKENS
     keys_paged = key_piece.reshape(piece_pages, PAGE_TOKENS, kv_heads, HEAD_SIZE).transpose(

time: 373 us -> 341 us (0.914)
  waiting for transfers between devices: 118 us -> 84.2 us
    all_gather x2 -> x1, waiting for transfers between devices: 72.6 us -> 41.5 us  [body(): lax.all_gather(jnp.concatenate([x_local, block_in], 1), axis_name=device_...]
  transfers between devices with their start and end apart: 6 -> 5, of which waited for: 5 -> 4; matrix products, arithmetic and copies ran while one was open for 7% -> 9% of each run, Pallas kernels for 0% -> 0%
where the time goes in v1:
time: 341 us; the launch traced here: 340 us
  matrix products  111 us (33%)
  waiting for transfers between devices  84.2 us (25%)
  blocking collectives  48.7 us (14%)
  other arithmetic  47.9 us (14%)
  local copies, waits for them, and re-layouts  32.9 us (10%)
  between operations  15.3 us (4%)
    all_gather x1, blocking collectives, body(): all_segs = lax.all_gather(seg_ids, ('req', 'ep'), axis=0, tiled=True)  43.2 us
    all_gather x1, waiting for transfers between devices, body(): lax.all_gather(jnp.concatenate([x_local, block_in], 1), axis_name=device_...  41.5 us
    dot_general x4, matrix products, one_block(): jnp.einsum('grqk,kgd->grqd', exponent.astype(jnp.bfloat16), value_block,...  30.3 us
    reduce_scatter x1, waiting for transfers between devices, body(): lax.psum_scatter(jnp.dot(head_out, w_out_attn, preferred_element_type=jnp...  26.8 us
    dot_general x4, matrix products, one_block(): jnp.einsum('grqd,kgd->grqk', query_grouped, key_block, preferred_element_...  26.7 us
    reduce_sum x4, other arithmetic, one_block(): new_sum = block_sum * rescale + jnp.sum(exponent, axis=-1)  26.2 us
    dot_general x1, matrix products, body(): jnp.einsum('esd,edf->esf', arrived, w_in, preferred_element_type=jnp.floa...  17.3 us
    dot_general x1, matrix products, body(): jnp.einsum('esr,esd->rd', dispatch.astype(jnp.float32), weighted, precisi...  15.5 us
  transfers between devices with their start and end apart: 5, of which 4 were waited for; matrix products, arithmetic and copies ran while one was open for 9% of the time, Pallas kernels for 0%

profile of v1, /device:TPU:0, one launch (start us, length us, event | category | flops | bytes accessed | tf_op | source)
XLA Modules:
  0.0 340.5 jit_solution(5574905531903767057)
XLA Ops:
  7.2 1.2 fusion.57
  8.5 1.9 fusion.59
  10.5 43.2 %all-gather = s32[32,1,128]{2,1,0:T(1,128)S(1)} all-gather(s32[1,1,128]{2,1,0:T(1,128)} %bitcast.111), channel_id=1, replica_groups=mesh['req'=8,'ep'=4] {'req','ep'}, dimensions={0}, use_global_device_ids=true | all-gather | bytes 16896 | tf_op jit(solution)/shard_map/all_gather | solution.py:68
  54.8 3.4 fusion.42
  58.2 1.0 copy-done.3
  62.8 1.2 slice.62
  64.5 41.5 %all-gather.7.cloned.1.call-done = bf16[4096,256]{1,0:T(8,128)(2,1)} async-done(((bf16[512,256]{1,0:T(8,128)(2,1)}), bf16[4096,256]{1,0:T(8,128)(2,1)}) %all-gather.7.cloned.1.call-update) | async-done | bytes 2097168 | tf_op jit(solution)/shard_map/all_gather | solution.py:114
  105.9 3.0 fusion.66
  108.9 96.9 %conditional.1 = (f32[2,3,512]{2,1,0:T(4,128)}, f32[2,3,512,64]{2,3,1,0:T(8,128)}) conditional(s32[]{:T(128)} %convert_element_type.66, () %tuple.30, (s32[]{:T(128)}, s32[512]{0:T(512)S(1)}, s32[512]{0:T(512)S(1)}, s32[4096]{0:T(1024)S(1)}, bf16[4096,128]{1,0:T(8,128)(2,1)}, /*index=5*/bf16[2,3,512,64]{2,3,1,0:T(8,128)(2,1)S(1)}, ...), branch_computations={%region_3.4_spmd, %region_4.9_spmd} | conditional | flops 848380416 | bytes 44659036 | solution.py:178
  108.9 96.9 %while.17 = (s32[]{:T(128)}, f32[2,3,512]{2,1,0:T(4,128)S(1)}, f32[2,3,512]{2,1,0:T(4,128)}, f32[2,3,512,64]{2,3,1,0:T(8,128)}, s32[512]{0:T(512)S(1)}, /*index=...) while((s32[]{:T(128)}, f32[2,3,512]{2,1,0:T(4,128)S(1)}, ...), condition=%wide.region_8.8_spmd.clone, body=%wide.region_5.7_spmd.clone.sunk | while | flops 848379904 | bytes 44654800 | solution.py:176
  109.8 1.1 constant_dynamic-slice_fusion.3
  111.0 6.7 %fusion.88 = (f32[2,3,512]{2,1,0:T(4,128)S(1)}, f32[2,1024,3,512]{3,1,2,0:T(8,128)}) fusion(pred[512,1024]{0,1:T(8,128)(4,1)S(1)} %compare_and_fusion.2, bf16[1024,2,64,1]{0,2,3,1:T(8,128)(2,1)S(1)} %bitcast.96, bf16[2,3,512,64]{2,3,1,0:T(8,128)(2,1)S(1)} %get-tuple-element.408), kind=kOutput, calls=%fused_computation.2.clone.1 | convolution fusion | flops 412087296 | bytes 13774848 | tf_op jit(solution)/shard_map/cond/branch_1_fun/while/body/eval_jaxpr/grqd,kgd->grqk/dot_general | solution.py:158
  117.7 6.5 %fusion.89 = f32[2,3,512]{2,1,0:T(4,128)S(1)} fusion(f32[2,1024,3,512]{3,1,2,0:T(8,128)} %get-tuple-element.368, f32[2,3,512]{2,1,0:T(4,128)S(1)} %select_maximum_fusion.2, pred[512,1024]{0,1:T(8,128)(4,1)S(1)} %compare_and_fusion.2), kind=kLoop, calls=%fused_computation.4.clone.1 | loop fusion | flops 15725568 | bytes 13131776 | tf_op jit(solution)/shard_map/cond/branch_1_fun/while/body/eval_jaxpr/reduce_sum | solution.py:167
  125.1 7.4 %fusion.91 = f32[2,3,512,64]{2,3,1,0:T(8,128)} fusion(bf16[1024,2,64,1]{0,2,3,1:T(8,128)(2,1)S(1)} %bitcast.97, f32[2,1024,3,512]{3,1,2,0:T(8,128)} %get-tuple-element.368, f32[2,3,512]{2,1,0:T(4,128)S(1)} %select_maximum_fusion.2, pred[512,1024]{0,1:T(8,128)(4,1)S(1)} %compare_and_fusion.2, f32[2,3,512,64]{2,3,1,0:T(8,128)} %get-tuple-element.389, ...), kind=kOutput, calls=%fused_computation.8.clone.1 | convolution fusion | flops 418971648 | bytes 14966785 | tf_op jit(solution)/shard_map/cond/branch_1_fun/while/body/eval_jaxpr/grqk,kgd->grqd/dot_general | solution.py:168
  133.3 1.1 constant_dynamic-slice_fusion.3
  134.5 6.7 %fusion.88 = (f32[2,3,512]{2,1,0:T(4,128)S(1)}, f32[2,1024,3,512]{3,1,2,0:T(8,128)}) fusion(pred[512,1024]{0,1:T(8,128)(4,1)S(1)} %compare_and_fusion.2, bf16[1024,2,64,1]{0,2,3,1:T(8,128)(2,1)S(1)} %bitcast.96, bf16[2,3,512,64]{2,3,1,0:T(8,128)(2,1)S(1)} %get-tuple-element.408), kind=kOutput, calls=%fused_computation.2.clone.1 | convolution fusion | flops 412087296 | bytes 13774848 | tf_op jit(solution)/shard_map/cond/branch_1_fun/while/body/eval_jaxpr/grqd,kgd->grqk/dot_general | solution.py:158
  141.2 6.5 %fusion.89 = f32[2,3,512]{2,1,0:T(4,128)S(1)} fusion(f32[2,1024,3,512]{3,1,2,0:T(8,128)} %get-tuple-element.368, f32[2,3,512]{2,1,0:T(4,128)S(1)} %select_maximum_fusion.2, pred[512,1024]{0,1:T(8,128)(4,1)S(1)} %compare_and_fusion.2), kind=kLoop, calls=%fused_computation.4.clone.1 | loop fusion | flops 15725568 | bytes 13131776 | tf_op jit(solution)/shard_map/cond/branch_1_fun/while/body/eval_jaxpr/reduce_sum | solution.py:167
  147.8 1.4 fusion.90
  149.3 7.6 %fusion.91 = f32[2,3,512,64]{2,3,1,0:T(8,128)} fusion(bf16[1024,2,64,1]{0,2,3,1:T(8,128)(2,1)S(1)} %bitcast.97, f32[2,1024,3,512]{3,1,2,0:T(8,128)} %get-tuple-element.368, f32[2,3,512]{2,1,0:T(4,128)S(1)} %select_maximum_fusion.2, pred[512,1024]{0,1:T(8,128)(4,1)S(1)} %compare_and_fusion.2, f32[2,3,512,64]{2,3,1,0:T(8,128)} %get-tuple-element.389, ...), kind=kOutput, calls=%fused_computation.8.clone.1 | convolution fusion | flops 418971648 | bytes 14966785 | tf_op jit(solution)/shard_map/cond/branch_1_fun/while/body/eval_jaxpr/grqk,kgd->grqd/dot_general | solution.py:168
  157.8 1.1 constant_dynamic-slice_fusion.3
  159.0 6.7 %fusion.88 = (f32[2,3,512]{2,1,0:T(4,128)S(1)}, f32[2,1024,3,512]{3,1,2,0:T(8,128)}) fusion(pred[512,1024]{0,1:T(8,128)(4,1)S(1)} %compare_and_fusion.2, bf16[1024,2,64,1]{0,2,3,1:T(8,128)(2,1)S(1)} %bitcast.96, bf16[2,3,512,64]{2,3,1,0:T(8,128)(2,1)S(1)} %get-tuple-element.408), kind=kOutput, calls=%fused_computation.2.clone.1 | convolution fusion | flops 412087296 | bytes 13774848 | tf_op jit(solution)/shard_map/cond/branch_1_fun/while/body/eval_jaxpr/grqd,kgd->grqk/dot_general | solution.py:158
  165.7 6.5 %fusion.89 = f32[2,3,512]{2,1,0:T(4,128)S(1)} fusion(f32[2,1024,3,512]{3,1,2,0:T(8,128)} %get-tuple-element.368, f32[2,3,512]{2,1,0:T(4,128)S(1)} %select_maximum_fusion.2, pred[512,1024]{0,1:T(8,128)(4,1)S(1)} %compare_and_fusion.2), kind=kLoop, calls=%fused_computation.4.clone.1 | loop fusion | flops 15725568 | bytes 13131776 | tf_op jit(solution)/shard_map/cond/branch_1_fun/while/body/eval_jaxpr/reduce_sum | solution.py:167
  172.2 1.4 fusion.90
  173.7 7.6 %fusion.91 = f32[2,3,512,64]{2,3,1,0:T(8,128)} fusion(bf16[1024,2,64,1]{0,2,3,1:T(8,128)(2,1)S(1)} %bitcast.97, f32[2,1024,3,512]{3,1,2,0:T(8,128)} %get-tuple-element.368, f32[2,3,512]{2,1,0:T(4,128)S(1)} %select_maximum_fusion.2, pred[512,1024]{0,1:T(8,128)(4,1)S(1)} %compare_and_fusion.2, f32[2,3,512,64]{2,3,1,0:T(8,128)} %get-tuple-element.389, ...), kind=kOutput, calls=%fused_computation.8.clone.1 | convolution fusion | flops 418971648 | bytes 14966785 | tf_op jit(solution)/shard_map/cond/branch_1_fun/while/body/eval_jaxpr/grqk,kgd->grqd/dot_general | solution.py:168
  182.2 1.1 constant_dynamic-slice_fusion.3
  183.4 6.7 %fusion.88 = (f32[2,3,512]{2,1,0:T(4,128)S(1)}, f32[2,1024,3,512]{3,1,2,0:T(8,128)}) fusion(pred[512,1024]{0,1:T(8,128)(4,1)S(1)} %compare_and_fusion.2, bf16[1024,2,64,1]{0,2,3,1:T(8,128)(2,1)S(1)} %bitcast.96, bf16[2,3,512,64]{2,3,1,0:T(8,128)(2,1)S(1)} %get-tuple-element.408), kind=kOutput, calls=%fused_computation.2.clone.1 | convolution fusion | flops 412087296 | bytes 13774848 | tf_op jit(solution)/shard_map/cond/branch_1_fun/while/body/eval_jaxpr/grqd,kgd->grqk/dot_general | solution.py:158
  190.1 6.5 %fusion.89 = f32[2,3,512]{2,1,0:T(4,128)S(1)} fusion(f32[2,1024,3,512]{3,1,2,0:T(8,128)} %get-tuple-element.368, f32[2,3,512]{2,1,0:T(4,128)S(1)} %select_maximum_fusion.2, pred[512,1024]{0,1:T(8,128)(4,1)S(1)} %compare_and_fusion.2), kind=kLoop, calls=%fused_computation.4.clone.1 | loop fusion | flops 15725568 | bytes 13131776 | tf_op jit(solution)/shard_map/cond/branch_1_fun/while/body/eval_jaxpr/reduce_sum | solution.py:167
  196.7 1.4 fusion.90
  198.2 7.6 %fusion.91 = f32[2,3,512,64]{2,3,1,0:T(8,128)} fusion(bf16[1024,2,64,1]{0,2,3,1:T(8,128)(2,1)S(1)} %bitcast.97, f32[2,1024,3,512]{3,1,2,0:T(8,128)} %get-tuple-element.368, f32[2,3,512]{2,1,0:T(4,128)S(1)} %select_maximum_fusion.2, pred[512,1024]{0,1:T(8,128)(4,1)S(1)} %compare_and_fusion.2, f32[2,3,512,64]{2,3,1,0:T(8,128)} %get-tuple-element.389, ...), kind=kOutput, calls=%fused_computation.8.clone.1 | convolution fusion | flops 418971648 | bytes 14966785 | tf_op jit(solution)/shard_map/cond/branch_1_fun/while/body/eval_jaxpr/grqk,kgd->grqd/dot_general | solution.py:168
  205.8 1.3 divide_convert_fusion
  207.1 2.2 convolution_convert_fusion.1
  209.4 26.8 %reduce-scatter.3.cloned.1.call-done = bf16[128,1536]{1,0:T(8,128)(2,1)} async-done(((bf16[512,1536]{1,0:T(8,128)(2,1)}), bf16[128,1536]{1,0:T(8,128)(2,1)}) %reduce-scatter.3.cloned.1.call-update) | async-done | bytes 393232 | tf_op jit(solution)/shard_map/reduce_scatter | solution.py:185
  236.1 1.2 multiply_reduce_fusion
  237.4 1.9 multiply_convert_fusion
  239.4 5.5 %all_gather.18 = f32[512,40]{0,1:T(8,128)S(1)} all-gather(f32[128,40]{0,1:T(8,128)S(1)} %select_reduce_fusion.1), channel_id=1, replica_groups=mesh['req'=8,'ep'=4] {'ep'}, dimensions={0}, use_global_device_ids=true | all-gather | bytes 102400 | tf_op jit(solution)/shard_map/all_gather | solution.py:203
  246.6 12.5 %all-gather.9.cloned.1.call-done = bf16[512,1536]{1,0:T(8,128)(2,1)} async-done(((bf16[128,1536]{1,0:T(8,128)(2,1)}), bf16[512,1536]{1,0:T(8,128)(2,1)}) %all-gather.9.cloned.1.call-update) | async-done | bytes 1572880 | tf_op jit(solution)/shard_map/all_gather | solution.py:202
  259.1 17.3 %fusion.19 = f32[10,192,1024]{2,1,0:T(8,128)} fusion(bf16[10,1536,1024]{2,1,0:T(8,128)(2,1)} %param.28, s32[10,512]{1,0:T(8,128)S(1)} %copy.60, pred[10,512]{1,0:T(8,128)(4,1)S(1)} %get-tuple-element.283, bf16[512,1536]{1,0:T(8,128)(2,1)} %all-gather.9.cloned.1.call-done), kind=kOutput, calls=%fused_computation.28 | convolution fusion | flops 9064611840 | bytes 40920064 | tf_op jit(solution)/shard_map/esd,edf->esf/dot_general | solution.py:217
  276.4 13.6 %fusion.40 = bf16[10,192,1536]{2,1,0:T(8,128)(2,1)} fusion(bf16[10,512,1536]{2,1,0:T(8,128)(2,1)} %param.29, f32[10,192,1024]{2,1,0:T(8,128)} %fusion.19), kind=kOutput, calls=%fused_computation.42 | convolution fusion | flops 3025797120 | bytes 29491200 | tf_op jit(solution)/shard_map/esf,efd->esd/dot_general | solution.py:221
  290.0 15.5 %fusion.35 = bf16[512,1536]{1,0:T(8,128)(2,1)} fusion(f32[10,192]{1,0:T(8,128)S(1)} %select_reduce_fusion, bf16[10,192,1536]{2,1,0:T(8,128)(2,1)} %fusion.40, s32[10,512]{1,0:T(8,128)S(1)} %copy.60, pred[10,512]{1,0:T(8,128)(4,1)S(1)} %get-tuple-element.283), kind=kOutput, calls=%fused_computation.38 | convolution fusion | flops 18128044032 | bytes 7504384 | tf_op jit(solution)/shard_map/esr,esd->rd/dot_general | solution.py:226
  305.6 1.9 reshape.181
  307.7 5.0 %reshape.179 = bf16[64,64,2,64]{3,2,1,0:T(2,128)(2,1)} reshape(bf16[4096,128]{1,0:T(8,128)(2,1)} %get-tuple-element.289) | data formatting | bytes 2097152 | tf_op jit(solution)/shard_map/reshape | solution.py:126
  312.8 1.8 reshape.178
  314.6 3.5 %copy_bitcast_fusion = (bf16[64,2,1,64,64]{4,3,2,1,0:T(8,128)(2,1)S(1)}, bf16[64,2,1,64,64]{4,3,2,1,0:T(8,128)(2,1)S(1)}) fusion(bf16[64,64,2,64]{3,2,1,0:T(2,128)(2,1)} %reshape.179, bf16[64,64,2,64]{3,2,1,0:T(2,128)(2,1)} %reshape.178), kind=kLoop, calls=%fused_computation.40 | loop fusion | bytes 4194304 | tf_op jit(solution)/shard_map/stack | solution.py:129
  318.1 2.7 pad_maximum_fusion
  320.8 6.0 %reshape.180 = bf16[64,16384]{1,0:T(8,128)(2,1)} reshape(bf16[64,2,2,64,64]{4,3,2,1,0:T(8,128)(2,1)} %pad_maximum_fusion) | data formatting | bytes 4194304 | tf_op jit(solution)/shard_map/reshape | solution.py:129
  326.8 2.1 fusion.13
  328.9 1.7 reshape.182
  330.6 3.3 reduce-scatter.5.cloned.1.call-done
  (97 shorter events, 11.1 us)
Async XLA Ops:
  7.2 199.9 %copy-start = (bf16[384,1536]{1,0:T(8,128)(2,1)S(1)}, bf16[384,1536]{1,0:T(8,128)(2,1)}, u32[]{:S(2)}) copy-start(bf16[384,1536]{1,0:T(8,128)(2,1)} %param.27) | copy-start | bytes 3538948
  7.2 47.6 %all-gather.5.cloned.1.call-start = ((), (), s32[]{:S(2)}) async-start(), calls=%async_computation.2 | async-start | bytes 1966080 | tf_op jit(solution)/shard_map/all_gather | solution.py:76
  10.4 95.5 %all-gather.7.cloned.1.call-start = ((), (), s32[]{:S(2)}) async-start(), calls=%async_computation.3 | async-start | bytes 2359296 | tf_op jit(solution)/shard_map/all_gather | solution.py:114
  58.2 1.1 copy-start.3
  60.4 175.8 %reduce-scatter.3.cloned.1.call-start = ((), (), s32[]{:S(2)}) async-start(), calls=%async_computation.4 | async-start | bytes 1966080 | tf_op jit(solution)/shard_map/reduce_scatter | solution.py:185
  205.8 30.3 %copy-start.2 = (bf16[128,1536]{1,0:T(8,128)(2,1)S(1)}, bf16[128,1536]{1,0:T(8,128)(2,1)}, u32[]{:S(2)}) copy-start(bf16[128,1536]{1,0:T(8,128)(2,1)} %param.18) | copy-start | bytes 1179652
  205.8 31.6 %copy-start.4 = (f32[1536]{0:T(1024)S(1)}, f32[1536]{0:T(1024)}, u32[]{:S(2)}) copy-start(f32[1536]{0:T(1024)} %param.23) | copy-start | bytes 18436
  205.8 33.6 %copy-start.5 = (f32[128,8]{0,1:T(8,128)S(1)}, f32[128,8]{0,1:T(8,128)}, u32[]{:S(2)}) copy-start(f32[128,8]{0,1:T(8,128)} %param.21) | copy-start | bytes 12292
  205.8 33.6 %copy-start.6 = (s32[128,8]{0,1:T(8,128)S(1)}, s32[128,8]{0,1:T(8,128)}, u32[]{:S(2)}) copy-start(s32[128,8]{0,1:T(8,128)} %param.20) | copy-start | bytes 12292
  209.3 49.8 %all-gather.9.cloned.1.call-start = ((), (), s32[]{:S(2)}) async-start(), calls=%async_computation.5 | async-start | bytes 1966080 | tf_op jit(solution)/shard_map/all_gather | solution.py:202
  239.3 94.6 %reduce-scatter.5.cloned.1.call-start = ((), (), s32[]{:S(2)}) async-start(), calls=%async_computation.6 | async-start | bytes 1966080 | tf_op jit(solution)/shard_map/reduce_scatter | solution.py:233
  290.0 17.5 %copy-start.7 = (s32[64]{0:T(128)S(1)}, s32[64]{0:T(128)}, u32[]{:S(2)}) copy-start(s32[64]{0:T(128)} %param.31) | copy-start | bytes 772
  305.6 7.2 %copy-start.1 = (bf16[4096,128]{1,0:T(8,128)(2,1)S(1)}, bf16[4096,128]{1,0:T(8,128)(2,1)}, u32[]{:S(2)}) copy-start(bf16[4096,128]{1,0:T(8,128)(2,1)} %get-tuple-element.290) | copy-start | bytes 3145732
Sparse Core Ops, SparseCore 0:
  10.5 22.3 all-gather.4
  60.5 45.3 all-gather.6
  209.4 26.6 reduce-scatter.2
  239.4 19.6 all-gather.8
  305.7 28.1 reduce-scatter.4
